TPU v7x, 32 devices: a whole 2x2x4 slice. The times are simulated.
32 devices in a mesh: row: 4 (over z), col: 4 (over y, core), pix: 2 (over x).
Axes of the slice: x: 2, y: 2, z: 4, core: 2. Of those that a mesh axis runs over, the one named last changes fastest.
Arguments:
- sample_frames: bfloat16 [4096, 16384], P(('row', 'col'), 'pix'), may hold values from 0.14 to 26
- reference_frames: bfloat16 [4096, 16384], P(('row', 'col'), 'pix'), may hold values from 0.14 to 26
- gain: float32 [16384], P('pix'), may hold values from 0.5 to 2
- flat: float32 [16384], P('pix'), may hold values from 0.6 to 1.6
- qbin: int32 [16384], P('pix'), may hold values from 0 to 31
- region: int32 [16384], P('pix'), may hold values 0 or 1
- live: int32 [16384], P('pix'), may hold values 0 or 1
Outputs:
- twotime: float32 [4096, 4, 4, 256], P('row', None, 'col', 'pix')
All inputs are finite; a program needn't handle non-finite values. No bound on the sum of `region` or of `live` on one device may be relied on, other than what follows from the above.
Results may differ from a plain program's by a relative error of at most 0.0039.
Values may be sent and summed in bfloat16 or wider, within the bound.
No kernel may reach another device: no remote copies, remote signals or barrier semaphores. Data moves between devices by JAX's collectives and lax.ppermute only.
A program may use at most 128 MiB of HBM per device.

v0:
```python
import math
import jax
import jax.numpy as jnp
from jax import lax
from jax.sharding import PartitionSpec as P

QBINS = 32


def on_device(sample_frames, reference_frames, gain, flat, qbin, region, live):
    block = sample_frames.shape[0]
    factor = gain / flat
    select = (qbin[None, :] == jnp.arange(QBINS, dtype=jnp.int32)[:, None]).astype(jnp.float32)
    ref_select = select * (live * (1 - region)).astype(jnp.float32)[None, :]
    sample_weight = (live * region).astype(jnp.float32)
    corrected_sample = sample_frames.astype(jnp.float32) * factor
    corrected_reference = reference_frames.astype(jnp.float32) * factor
    sums_sample = jnp.dot(corrected_sample, ref_select.T, precision=lax.Precision.HIGHEST)
    sums_reference = jnp.dot(corrected_reference, ref_select.T, precision=lax.Precision.HIGHEST)
    counts = jnp.sum(ref_select, axis=1)
    sums_sample, sums_reference, counts = lax.psum((sums_sample, sums_reference, counts), "pix")
    mean_sample = (sums_sample + 1.0) / (counts + 1.0)
    mean_reference = (sums_reference + 1.0) / (counts + 1.0)
    spread_sample = jnp.dot(mean_sample, select, precision=lax.Precision.HIGHEST)
    spread_reference = jnp.dot(mean_reference, select, precision=lax.Precision.HIGHEST)
    delta_sample = ((corrected_sample / spread_sample - 1.0) * sample_weight).astype(jnp.bfloat16)
    delta_reference = (corrected_reference / spread_reference - 1.0).astype(jnp.bfloat16)
    sample_rows = lax.all_gather(delta_sample, "col", axis=0, tiled=True)
    partial_value = lax.dot_general(
        sample_rows,
        lax.all_gather(delta_reference, "row", axis=0, tiled=True),
        (((1,), (1,)), ((), ())),
        preferred_element_type=jnp.float32,
    )
    groups = lax.axis_size("row")
    scale = 1.0 / math.sqrt(gain.shape[0] * lax.axis_size("pix"))
    partial_value = (partial_value * scale).reshape(sample_rows.shape[0], groups, block)
    whole = lax.psum(partial_value, "pix")
    width = block // lax.axis_size("pix")
    mine = lax.dynamic_slice_in_dim(whole, lax.axis_index("pix") * width, width, 2)
    return mine[:, :, None, :]


def solution(mesh):
    return jax.shard_map(
        on_device,
        mesh=mesh,
        in_specs=(
            P(("row", "col"), "pix"),
            P(("row", "col"), "pix"),
            P("pix"),
            P("pix"),
            P("pix"),
            P("pix"),
            P("pix"),
        ),
        out_specs=P("row", None, "col", "pix"),
        check_vma=False,
    )
```

profile of v0, /device:TPU:0, one launch (start us, length us, event | category | flops | bytes accessed | tf_op | source)
XLA Modules:
  0.0 598.4 jit_solution(18286605986021742596)
XLA Ops:
  6.5 0.0 all-reduce.6.cloned.1.call-start
  6.5 0.8 multiply_convert_fusion.1
  7.3 0.8 div.23
  8.1 1.5 select_reduce_fusion
  9.6 9.2 %fusion.5 = f32[256,32]{1,0:T(8,128)} fusion(bf16[256,8192]{1,0:T(8,128)(2,1)} %param.8, f32[8192]{0:T(1024)S(1)} %div.23, f32[8192]{0:T(1024)S(1)} %get-tuple-element.8, s32[8192]{0:T(1024)} %param.11), kind=kOutput, calls=%fused_computation.8 | convolution fusion | flops 810024960 | bytes 4325376 | tf_op jit(solution)/shard_map/dot_general | solution.py:19
  18.8 9.2 %fusion.6 = f32[256,32]{1,0:T(8,128)} fusion(bf16[256,8192]{1,0:T(8,128)(2,1)} %param.7, f32[8192]{0:T(1024)S(1)} %div.23, f32[8192]{0:T(1024)S(1)} %get-tuple-element.8, s32[8192]{0:T(1024)} %param.11), kind=kOutput, calls=%fused_computation.10 | convolution fusion | flops 810024960 | bytes 4325376 | tf_op jit(solution)/shard_map/dot_general | solution.py:18
  28.0 0.0 all-reduce.6.cloned.1.call-update
  28.1 0.0 all-gather.3.cloned.1.call-start
  28.1 26.4 %all-reduce.6.cloned.1.call-done = (f32[256,32]{1,0:T(8,128)}, f32[32]{0:T(128)}, f32[256,32]{1,0:T(8,128)}) async-done(((f32[256,32]{1,0:T(8,128)}, f32[32]{0:T(128)}, f32[256,32]{1,0:T(8,128)}), (f32[256,32]{1,0:T(8,128)}, f32[32]{0:T(128)}, f32[256,32]{1,0:T(8,128)})) %all-reduce.6.cloned.1.call-update) | async-done | bytes 65680 | tf_op jit(solution)/shard_map/psum | solution.py:21
  54.5 0.6 broadcast_add_fusion
  55.1 0.0 copy-done
  55.1 7.9 %fusion.4 = bf16[256,8192]{1,0:T(8,128)(2,1)} fusion(bf16[256,8192]{1,0:T(8,128)(2,1)} %param.7, f32[8192]{0:T(1024)S(1)} %get-tuple-element.9, f32[8192]{0:T(1024)S(1)} %div.23, s32[8192]{0:T(1024)S(1)} %copy-done, f32[256,32]{1,0:T(8,128)} %get-tuple-element.5, f32[32]{0:T(128)S(1)} %broadcast_add_fusion), kind=kOutput, calls=%fused_computation.6 | convolution fusion | flops 818167808 | bytes 8519808 | tf_op jit(solution)/shard_map/dot_general | solution.py:24
  63.0 0.0 all-gather.3.cloned.1.call-update
  63.0 0.2 all-gather.5.cloned.1.call-start
  63.3 7.6 %fusion.1 = bf16[256,8192]{1,0:T(8,128)(2,1)} fusion(bf16[256,8192]{1,0:T(8,128)(2,1)} %param.8, f32[8192]{0:T(1024)S(1)} %div.23, s32[8192]{0:T(1024)S(1)} %copy-done, f32[256,32]{1,0:T(8,128)S(1)} %copy-done.1, f32[32]{0:T(128)S(1)} %broadcast_add_fusion), kind=kOutput, calls=%fused_computation.2 | convolution fusion | flops 816070656 | bytes 8487040 | tf_op jit(solution)/shard_map/dot_general | solution.py:25
  70.9 0.0 all-gather.5.cloned.1.call-update
  70.9 0.0 all-reduce.4.cloned.1.call-start
  70.9 98.4 %all-gather.3.cloned.1.call-done = bf16[1024,8192]{1,0:T(8,128)(2,1)} async-done(((bf16[256,8192]{1,0:T(8,128)(2,1)}), bf16[1024,8192]{1,0:T(8,128)(2,1)}) %all-gather.3.cloned.1.call-update) | async-done | bytes 16777232 | tf_op jit(solution)/shard_map/all_gather | solution.py:28
  169.3 288.5 %all-gather.5.cloned.1.call-done = bf16[1024,8192]{1,0:T(8,128)(2,1)} async-done(((bf16[256,8192]{1,0:T(8,128)(2,1)}), bf16[1024,8192]{1,0:T(8,128)(2,1)}) %all-gather.5.cloned.1.call-update) | async-done | bytes 16777232 | tf_op jit(solution)/shard_map/all_gather | solution.py:31
  457.8 24.3 %convolution_multiply_fusion = f32[1024,1024]{0,1:T(8,128)} fusion(bf16[1024,8192]{1,0:T(8,128)(2,1)} %all-gather.3.cloned.1.call-done, bf16[1024,8192]{1,0:T(8,128)(2,1)} %all-gather.5.cloned.1.call-done), kind=kOutput, calls=%fused_computation.13 | convolution fusion | flops 17180917760 | bytes 37748736 | tf_op jit(solution)/shard_map/dot_general | solution.py:29
  482.1 0.0 all-reduce.4.cloned.1.call-update
  482.1 106.2 %all-reduce.4.cloned.1.call-done = f32[1024,4,256]{0,2,1:T(8,128)} async-done(((f32[1024,4,256]{0,2,1:T(8,128)}), f32[1024,4,256]{0,2,1:T(8,128)}) %all-reduce.4.cloned.1.call-update) | async-done | bytes 4194320 | tf_op jit(solution)/shard_map/psum | solution.py:38
  588.3 1.7 constant_dynamic-slice_fusion
  590.1 1.8 copy.9
  (3 shorter events, 0.0 us)
Async XLA Ops:
  6.5 48.6 %copy-start = (s32[8192]{0:T(1024)S(1)}, s32[8192]{0:T(1024)}, u32[]{:S(2)}) copy-start(s32[8192]{0:T(1024)} %param.11) | copy-start | bytes 98308
  6.5 48.0 %all-reduce.6.cloned.1.call-start = ((), (), s32[]{:S(2)}) async-start(), calls=%async_computation.3 | async-start | bytes 525312 | tf_op jit(solution)/shard_map/psum | solution.py:21
  28.1 141.3 %all-gather.3.cloned.1.call-start = ((), (), s32[]{:S(2)}) async-start(), calls=%async_computation | async-start | bytes 20971520 | tf_op jit(solution)/shard_map/all_gather | solution.py:28
  55.1 8.2 %copy-start.1 = (f32[256,32]{1,0:T(8,128)S(1)}, f32[256,32]{1,0:T(8,128)}, u32[]{:S(2)}) copy-start(f32[256,32]{1,0:T(8,128)} %get-tuple-element.7) | copy-start | bytes 98308
  63.0 394.8 %all-gather.5.cloned.1.call-start = ((), (), s32[]{:S(2)}) async-start(), calls=%async_computation.1 | async-start | bytes 20971520 | tf_op jit(solution)/shard_map/all_gather | solution.py:31
  70.9 517.4 %all-reduce.4.cloned.1.call-start = ((), (), s32[]{:S(2)}) async-start(), calls=%async_computation.2 | async-start | bytes 8388608 | tf_op jit(solution)/shard_map/psum | solution.py:38
Sparse Core Ops, SparseCore 0:
  28.2 26.2 all-reduce.5
  63.2 106.1 all-gather.2
  171.0 286.7 all-gather.4
  482.3 106.0 all-reduce.3
where the time goes:
time: 599 us; the launch traced here: 598 us
  waiting for transfers between devices  519 us (87%)
  matrix products  58.3 us (10%)
  between operations  13.2 us (2%)
    all_gather x1, waiting for transfers between devices, on_device(): lax.all_gather(delta_reference, 'row', axis=0, tiled=True)  288 us
    psum x1, waiting for transfers between devices, on_device(): whole = lax.psum(partial_value, 'pix')  106 us
    all_gather x1, waiting for transfers between devices, on_device(): sample_rows = lax.all_gather(delta_sample, 'col', axis=0, tiled=True)  98.4 us
    psum x1, waiting for transfers between devices, on_device(): lax.psum((sums_sample, sums_reference, counts), 'pix')  26.4 us
    dot_general x1, matrix products, on_device(): lax.dot_general(sample_rows, lax.all_gather(delta_reference, 'row', axis=...  24.3 us
  transfers between devices with their start and end apart: 4, of which 4 were waited for; matrix products, arithmetic and copies ran while one was open for 1% of the time, Pallas kernels for 0%

commit v1 on v0

--- a/solution.py
+++ b/solution.py
@@ -5,6 +5,23 @@
 from jax.sharding import PartitionSpec as P
 
 QBINS = 32
+
+
+def in_order(blocks, dim):
+    dims = list(blocks.shape[1:])
+    dims[dim] *= blocks.shape[0]
+    return jnp.moveaxis(blocks, 0, dim).reshape(dims)
+
+
+def collect(array, axis, dim):
+    devices = lax.axis_size(axis)
+    upward = [(i, (i + 1) % devices) for i in range(devices)]
+    blocks = [array]
+    while len(blocks) < devices:
+        blocks.append(lax.ppermute(blocks[-1], axis, upward))
+    index = lax.axis_index(axis)
+    blocks = jnp.stack(blocks)[(index - jnp.arange(devices)) % devices]
+    return in_order(blocks, dim)
 
 
 def on_device(sample_frames, reference_frames, gain, flat, qbin, region, live):
@@ -28,7 +45,7 @@
     sample_rows = lax.all_gather(delta_sample, "col", axis=0, tiled=True)
     partial_value = lax.dot_general(
         sample_rows,
-        lax.all_gather(delta_reference, "row", axis=0, tiled=True),
+        collect(delta_reference, "row", 0),
         (((1,), (1,)), ((), ())),
         preferred_element_type=jnp.float32,
     )

time: 599 us -> 552 us (0.922)
  waiting for transfers between devices: 519 us -> 409 us
  other arithmetic: 3.66 us -> 37.4 us
  local copies, waits for them, and re-layouts: 3.55 us -> 34.5 us
    all_gather x1 -> x0, waiting for transfers between devices: 288 us -> none  [on_device(): lax.all_gather(delta_reference, 'row', axis=0, tiled=True)]
    ppermute x0 -> x3, waiting for transfers between devices: none -> 278 us  [collect(): blocks.append(lax.ppermute(blocks[-1], axis, upward))]
    all_gather x1, waiting for transfers between devices: 98.4 us -> 0.01 us  [on_device(): sample_rows = lax.all_gather(delta_sample, 'col', axis=0, tiled=True)]
    gather x0 -> x4, local copies, waits for them, and re-layouts: none -> 26.9 us  [collect(): blocks = jnp.stack(blocks)[(index - jnp.arange(devices)) % devices]]
    another operation x0 -> x1, other arithmetic: none -> 13.9 us  [collect(): blocks = jnp.stack(blocks)[(index - jnp.arange(devices)) % devices]]
    unnamed x0 -> x1, other arithmetic: none -> 13.7 us
  transfers between devices with their start and end apart: 4 -> 6, of which waited for: 4 -> 5; matrix products, arithmetic and copies ran while one was open for 1% -> 12% of each run, Pallas kernels for 0% -> 0%
where the time goes in v1:
time: 552 us
  waiting for transfers between devices  409 us (74%)
  matrix products  55.1 us (10%)
  other arithmetic  37.4 us (7%)
  local copies, waits for them, and re-layouts  34.5 us (6%)
  between operations  13.2 us (2%)
    ppermute x3, waiting for transfers between devices, collect(): blocks.append(lax.ppermute(blocks[-1], axis, upward))  278 us
    psum x1, waiting for transfers between devices, on_device(): whole = lax.psum(partial_value, 'pix')  105 us
    gather x4, local copies, waits for them, and re-layouts, collect(): blocks = jnp.stack(blocks)[(index - jnp.arange(devices)) % devices]  26.9 us
    psum x1, waiting for transfers between devices, on_device(): lax.psum((sums_sample, sums_reference, counts), 'pix')  26.2 us
    dot_general x1, matrix products, on_device(): lax.dot_general(sample_rows, collect(delta_reference, 'row', 0), (((1,),...  24.3 us
    another operation x1, other arithmetic, collect(): blocks = jnp.stack(blocks)[(index - jnp.arange(devices)) % devices]  13.9 us
    unnamed x1, other arithmetic  13.7 us
  transfers between devices with their start and end apart: 6, of which 5 were waited for; matrix products, arithmetic and copies ran while one was open for 12% of the time, Pallas kernels for 0%

profile of v1, /device:TPU:0, one launch (start us, length us, event | category | flops | bytes accessed | tf_op | source)
XLA Modules:
  0.0 551.5 jit_solution(4250039349875588054)
XLA Ops:
  7.5 1.1 div.23
  8.6 1.5 select_reduce_fusion
  10.1 9.2 %fusion.5 = f32[256,32]{1,0:T(8,128)} fusion(bf16[256,8192]{1,0:T(8,128)(2,1)} %param.8, f32[8192]{0:T(1024)S(1)} %div.23, f32[8192]{0:T(1024)S(1)} %get-tuple-element.10, s32[8192]{0:T(1024)} %param.11), kind=kOutput, calls=%fused_computation.13 | convolution fusion | flops 810024960 | bytes 4325376 | tf_op jit(solution)/shard_map/dot_general | solution.py:36
  19.4 7.3 %fusion.6 = f32[256,32]{1,0:T(8,128)} fusion(bf16[256,8192]{1,0:T(8,128)(2,1)S(1)} %copy-done.3, f32[8192]{0:T(1024)S(1)} %div.23, f32[8192]{0:T(1024)S(1)} %get-tuple-element.10, s32[8192]{0:T(1024)S(1)} %copy-done.2), kind=kOutput, calls=%fused_computation.15 | convolution fusion | flops 810024960 | bytes 4325376 | tf_op jit(solution)/shard_map/dot_general | solution.py:35
  26.9 26.2 %all-reduce.6.cloned.1.call-done = (f32[256,32]{1,0:T(8,128)}, f32[32]{0:T(128)}, f32[256,32]{1,0:T(8,128)}) async-done(((f32[256,32]{1,0:T(8,128)}, f32[32]{0:T(128)}, f32[256,32]{1,0:T(8,128)}), (f32[256,32]{1,0:T(8,128)}, f32[32]{0:T(128)}, f32[256,32]{1,0:T(8,128)})) %all-reduce.6.cloned.1.call-update) | async-done | bytes 65680 | tf_op jit(solution)/shard_map/psum | solution.py:38
  53.8 8.1 %fusion.4 = bf16[256,8192]{1,0:T(8,128)(2,1)} fusion(bf16[256,8192]{1,0:T(8,128)(2,1)} %param.7, f32[8192]{0:T(1024)S(1)} %get-tuple-element.11, f32[8192]{0:T(1024)S(1)} %div.23, s32[8192]{0:T(1024)S(1)} %copy-done.2, f32[256,32]{1,0:T(8,128)} %get-tuple-element.5, f32[32]{0:T(128)S(1)} %broadcast_add_fusion), kind=kOutput, calls=%fused_computation.11 | convolution fusion | flops 818167808 | bytes 8519808 | tf_op jit(solution)/shard_map/dot_general | solution.py:41
  61.9 6.2 %fusion.1 = bf16[256,8192]{1,0:T(8,128)(2,1)S(1)} fusion(bf16[256,8192]{1,0:T(8,128)(2,1)} %param.8, f32[8192]{0:T(1024)S(1)} %div.23, s32[8192]{0:T(1024)S(1)} %copy-done.2, f32[256,32]{1,0:T(8,128)S(1)} %copy-done.4, f32[32]{0:T(128)S(1)} %broadcast_add_fusion), kind=kOutput, calls=%fused_computation.7 | convolution fusion | flops 816070656 | bytes 8487040 | tf_op jit(solution)/shard_map/dot_general | solution.py:42
  68.2 2.1 copy-done
  70.3 1.5 collective-permute-start
  71.8 92.5 %collective-permute-done = bf16[256,8192]{1,0:T(8,128)(2,1)S(1)} collective-permute-done((bf16[256,8192]{1,0:T(8,128)(2,1)S(1)}, bf16[256,8192]{1,0:T(8,128)(2,1)S(1)}, u32[]{:S(2)}, u32[]{:S(2)}) %collective-permute-start) | collective-permute-done | bytes 4194336 | tf_op jit(solution)/shard_map/ppermute | solution.py:21
  164.3 2.0 copy-done.1
  166.2 93.1 %collective-permute-done.1 = bf16[256,8192]{1,0:T(8,128)(2,1)} collective-permute-done((bf16[256,8192]{1,0:T(8,128)(2,1)S(1)}, bf16[256,8192]{1,0:T(8,128)(2,1)}, u32[]{:S(2)}, u32[]{:S(2)}) %collective-permute-start.1) | collective-permute-done | bytes 4194336 | tf_op jit(solution)/shard_map/ppermute | solution.py:21
  259.4 92.4 %collective-permute-done.2 = bf16[256,8192]{1,0:T(8,128)(2,1)} collective-permute-done((bf16[256,8192]{1,0:T(8,128)(2,1)}, bf16[256,8192]{1,0:T(8,128)(2,1)}, u32[]{:S(2)}, u32[]{:S(2)}) %collective-permute-start.2) | collective-permute-done | bytes 4194336 | tf_op jit(solution)/shard_map/ppermute | solution.py:21
  351.8 13.9 %pad_maximum_fusion = bf16[4,256,8192]{2,1,0:T(8,128)(2,1)} fusion(bf16[1,256,8192]{2,1,0:T(8,128)(2,1)} %bitcast.3, bf16[1,256,8192]{2,1,0:T(8,128)(2,1)} %bitcast.2, bf16[1,256,8192]{2,1,0:T(8,128)(2,1)} %bitcast.14, bf16[1,256,8192]{2,1,0:T(8,128)(2,1)} %bitcast.12), kind=kLoop, calls=%fused_computation.3 | loop fusion | flops 25165824 | bytes 33554432 | tf_op jit(solution)/shard_map/stack | solution.py:23
  365.7 9.3 %fusion.33 = (bf16[4,256,2816]{2,1,0:T(8,128)(2,1)}, bf16[4,256,2816]{2,1,0:T(8,128)(2,1)}) fusion(bf16[4,256,8192]{2,1,0:T(8,128)(2,1)} %pad_maximum_fusion), kind=kLoop, calls=%fused_computation.55 | loop fusion | bytes 23068672 | tf_op jit(solution)/shard_map/gather | solution.py:23
  374.9 6.0 %gather_fusion = bf16[4,256,2816]{2,1,0:T(8,128)(2,1)} fusion(bf16[4,256,2816]{2,1,0:T(8,128)(2,1)} %get-tuple-element.8, s32[1024]{0:T(1024)S(1)} %pad_clamp_fusion), kind=kCustom, calls=%fused_computation | custom fusion | bytes 11534352 | tf_op jit(solution)/shard_map/gather | solution.py:23
  380.9 6.0 %gather_fusion.1 = bf16[4,256,2816]{2,1,0:T(8,128)(2,1)} fusion(bf16[4,256,2816]{2,1,0:T(8,128)(2,1)} %get-tuple-element.9, s32[1024]{0:T(1024)S(1)} %pad_clamp_fusion), kind=kCustom, calls=%fused_computation.1 | custom fusion | bytes 11534352 | tf_op jit(solution)/shard_map/gather | solution.py:23
  386.9 5.6 %pad_maximum_fusion.2 = bf16[4,256,2560]{2,1,0:T(8,128)(2,1)} fusion(bf16[1,256,8192]{2,1,0:T(8,128)(2,1)} %bitcast.3, bf16[1,256,8192]{2,1,0:T(8,128)(2,1)} %bitcast.2, bf16[1,256,8192]{2,1,0:T(8,128)(2,1)} %bitcast.15, bf16[1,256,8192]{2,1,0:T(8,128)(2,1)} %bitcast.13), kind=kLoop, calls=%fused_computation.16 | loop fusion | flops 20971520 | bytes 22020096 | tf_op jit(solution)/shard_map/gather | solution.py:23
  392.5 5.6 %gather_fusion.2 = bf16[4,256,2560]{2,1,0:T(8,128)(2,1)} fusion(bf16[4,256,2560]{2,1,0:T(8,128)(2,1)} %pad_maximum_fusion.2, s32[1024]{0:T(1024)S(1)} %pad_clamp_fusion), kind=kCustom, calls=%fused_computation.2 | custom fusion | bytes 10485776 | tf_op jit(solution)/shard_map/gather | solution.py:23
  398.1 13.7 %pad_maximum_fusion.1 = bf16[4,256,8192]{2,1,0:T(8,128)(2,1)} fusion(bf16[4,256,2560]{2,1,0:T(8,128)(2,1)} %gather_fusion.2, bf16[4,256,2816]{2,1,0:T(8,128)(2,1)} %gather_fusion.1, bf16[4,256,2816]{2,1,0:T(8,128)(2,1)} %gather_fusion), kind=kLoop, calls=%fused_computation.4 | loop fusion | flops 50331648 | bytes 33554432
  411.8 24.3 %convolution_multiply_fusion = f32[1024,1024]{0,1:T(8,128)} fusion(bf16[1024,8192]{1,0:T(8,128)(2,1)} %all-gather.2.cloned.1.call-done, bf16[1024,8192]{1,0:T(8,128)(2,1)} %bitcast.11), kind=kOutput, calls=%fused_computation.19 | convolution fusion | flops 17180917760 | bytes 37748736 | tf_op jit(solution)/shard_map/dot_general | solution.py:46
  436.2 105.3 %all-reduce.4.cloned.1.call-done = f32[1024,4,256]{0,2,1:T(8,128)} async-done(((f32[1024,4,256]{0,2,1:T(8,128)}), f32[1024,4,256]{0,2,1:T(8,128)}) %all-reduce.4.cloned.1.call-update) | async-done | bytes 4194320 | tf_op jit(solution)/shard_map/psum | solution.py:55
  541.4 1.7 constant_dynamic-slice_fusion
  543.2 1.8 copy.9
  (21 shorter events, 2.0 us)
Async XLA Ops:
  6.5 12.8 %copy-start.2 = (s32[8192]{0:T(1024)S(1)}, s32[8192]{0:T(1024)}, u32[]{:S(2)}) copy-start(s32[8192]{0:T(1024)} %param.11) | copy-start | bytes 98308
  6.5 46.6 %all-reduce.6.cloned.1.call-start = ((), (), s32[]{:S(2)}) async-start(), calls=%async_computation.2 | async-start | bytes 525312 | tf_op jit(solution)/shard_map/psum | solution.py:38
  6.5 12.8 %copy-start.3 = (bf16[256,8192]{1,0:T(8,128)(2,1)S(1)}, bf16[256,8192]{1,0:T(8,128)(2,1)}, u32[]{:S(2)}) copy-start(bf16[256,8192]{1,0:T(8,128)(2,1)} %param.7) | copy-start | bytes 12582916
  26.7 385.1 %all-gather.2.cloned.1.call-start = ((), (), s32[]{:S(2)}) async-start(), calls=%async_computation | async-start | bytes 20971520 | tf_op jit(solution)/shard_map/all_gather | solution.py:45
  53.8 8.1 %copy-start.4 = (f32[256,32]{1,0:T(8,128)S(1)}, f32[256,32]{1,0:T(8,128)}, u32[]{:S(2)}) copy-start(f32[256,32]{1,0:T(8,128)} %get-tuple-element.7) | copy-start | bytes 98308
  61.9 479.6 %all-reduce.4.cloned.1.call-start = ((), (), s32[]{:S(2)}) async-start(), calls=%async_computation.1 | async-start | bytes 8388608 | tf_op jit(solution)/shard_map/psum | solution.py:55
  68.2 2.1 copy-start
  70.3 93.9 %collective-permute-start = (bf16[256,8192]{1,0:T(8,128)(2,1)S(1)}, bf16[256,8192]{1,0:T(8,128)(2,1)S(1)}, u32[]{:S(2)}, u32[]{:S(2)}) collective-permute-start(bf16[256,8192]{1,0:T(8,128)(2,1)S(1)} %fusion.1), channel_id=1, source_target_pairs={{0,8},{8,16},{16,24},{24,0},{1,9},{9,17},{17,25},{25,1},{2,10},{10... | collective-permute-start | bytes 12582920 | tf_op jit(solution)/shard_map/ppermute | solution.py:21
  164.3 2.0 copy-start.1
  166.2 93.1 %collective-permute-start.1 = (bf16[256,8192]{1,0:T(8,128)(2,1)S(1)}, bf16[256,8192]{1,0:T(8,128)(2,1)}, u32[]{:S(2)}, u32[]{:S(2)}) collective-permute-start(bf16[256,8192]{1,0:T(8,128)(2,1)S(1)} %collective-permute-done), channel_id=1, source_target_pairs={{0,8},{8,16},{16,24},{24,0},{1,9},{9,17},{17,25},{25,1},{2,10},{10... | collective-permute-start | bytes 12582920 | tf_op jit(solution)/shard_map/ppermute | solution.py:21
  259.4 92.4 %collective-permute-start.2 = (bf16[256,8192]{1,0:T(8,128)(2,1)}, bf16[256,8192]{1,0:T(8,128)(2,1)}, u32[]{:S(2)}, u32[]{:S(2)}) collective-permute-start(bf16[256,8192]{1,0:T(8,128)(2,1)} %collective-permute-done.1), channel_id=1, source_target_pairs={{0,8},{8,16},{16,24},{24,0},{1,9},{9,17},{17,25},{25,1},{2,10},{10... | collective-permute-start | bytes 12582920 | tf_op jit(solution)/shard_map/ppermute | solution.py:21
Sparse Core Ops, SparseCore 0:
  26.8 26.2 all-reduce.5
  62.0 106.1 all-gather.1
  436.3 105.1 all-reduce.3
